TPU v7x, 32 devices: a whole 2x2x4 slice. The times are simulated.
32 devices in a mesh: dp: 4 (over y, core), mp: 8 (over z, x).
Axes of the slice: x: 2, y: 2, z: 4, core: 2. Of those that a mesh axis runs over, the one named last changes fastest.
Arguments:
- grad_part: bfloat16 [4, 24, 512, 512], P('dp', None, 'mp'), may hold values from -3 to 3
- owner: int32 [4, 6], replicated, may hold values from 0 to 7, as said below
- moment: bfloat16 [24, 512, 512], P('dp', 'mp'), may hold values from -6 to 6
- gram_left: bfloat16 [4, 8, 2, 512, 512], P('dp', 'mp'), may hold values from -1 to 7, as said below
- gram_right: bfloat16 [4, 8, 2, 512, 512], P('dp', 'mp'), may hold values from -1 to 7, as said below
- basis_left: bfloat16 [4, 8, 2, 512, 512], P('dp', 'mp'), may hold values from -1 to 2, as said below
- basis_right: bfloat16 [4, 8, 2, 512, 512], P('dp', 'mp'), may hold values from -1 to 2, as said below
Outputs:
- gram_left_new: bfloat16 [4, 8, 2, 512, 512], P('dp', 'mp')
- gram_right_new: bfloat16 [4, 8, 2, 512, 512], P('dp', 'mp')
- basis_left_new: bfloat16 [4, 8, 2, 512, 512], P('dp', 'mp')
- basis_right_new: bfloat16 [4, 8, 2, 512, 512], P('dp', 'mp')
- moment_new: bfloat16 [24, 512, 512], P('dp', 'mp')
Inputs may be any that keep to these rules, and one draw needn't show every extreme that they name: In every row, owners 2i and 2i + 1 together own at most 2 blocks, and some owner owns exactly 2 blocks. `gram_left`: each slot is symmetric positive definite. `gram_right`: each slot is symmetric positive definite. `basis_left`: each slot is nonsingular. `basis_right`: each slot is nonsingular.
All inputs are finite; a program needn't handle non-finite values.
Results may differ from a plain program's by a relative error of at most 0.008.
Values may be sent and summed in bfloat16 or wider, within the bound.
No kernel may reach another device: no remote copies, remote signals or barrier semaphores. Data moves between devices by JAX's collectives and lax.ppermute only.
A program may use at most 128 MiB of HBM per device.

v0:
```python
import jax
import jax.numpy as jnp
from jax import lax
from jax.sharding import PartitionSpec as P

gram_decay = 0.85
moment_decay = 0.9


def slot_numbers(row):
    length = row.shape[0]
    equal_owner = row[:, None] == row[None, :]
    earlier = lax.broadcasted_iota(jnp.int32, (length, length), 1) < lax.broadcasted_iota(
        jnp.int32, (length, length), 0
    )
    return jnp.sum(jnp.where(equal_owner & earlier, 1, 0), axis=1).astype(jnp.int32)


def slot_mapping(row, slot_count, owner_count):
    numbers = slot_numbers(row)
    by_owner = row[:, None, None] == lax.broadcasted_iota(jnp.int32, (1, 1, owner_count), 2)
    by_slot = numbers[:, None, None] == lax.broadcasted_iota(jnp.int32, (1, slot_count, 1), 1)
    return (by_owner & by_slot).astype(jnp.bfloat16)


def pack_rows(onehot, rows_in):
    spread = jnp.einsum("jso,jrc->sorc", onehot, rows_in, preferred_element_type=jnp.float32)
    return spread.astype(jnp.bfloat16).reshape(
        spread.shape[0], spread.shape[1] * spread.shape[2], spread.shape[3]
    )


def orthonormal(matrix_product):
    square = jnp.dot(
        matrix_product.T,
        matrix_product,
        precision=lax.Precision.HIGHEST,
        preferred_element_type=jnp.float32,
    )
    factor = jnp.linalg.cholesky(square)
    solved = jax.scipy.linalg.solve_triangular(factor, matrix_product.T, lower=True)
    return solved.T.astype(jnp.bfloat16)


def refresh(left_gram, right_gram, left_old, right_old, gradient, moment):
    block_width = gradient.shape[0]
    outer_left = jnp.dot(gradient, gradient.T, preferred_element_type=jnp.float32)
    outer_right = jnp.dot(gradient.T, gradient, preferred_element_type=jnp.float32)
    left_stat = (
        gram_decay * left_gram.astype(jnp.float32) + (1.0 - gram_decay) / block_width * outer_left
    ).astype(jnp.bfloat16)
    right_statistic = (
        gram_decay * right_gram.astype(jnp.float32) + (1.0 - gram_decay) / block_width * outer_right
    ).astype(jnp.bfloat16)
    left_basis = orthonormal(jnp.dot(left_stat, left_old, preferred_element_type=jnp.float32))
    right_basis = orthonormal(
        jnp.dot(right_statistic, right_old, preferred_element_type=jnp.float32)
    )
    restored = jnp.dot(left_old, moment, preferred_element_type=jnp.float32).astype(jnp.bfloat16)
    mixed = (
        moment_decay * jnp.dot(restored, right_old.T, preferred_element_type=jnp.float32)
        + (1.0 - moment_decay) * gradient.astype(jnp.float32)
    ).astype(jnp.bfloat16)
    turned = jnp.dot(left_basis.T, mixed, preferred_element_type=jnp.float32).astype(jnp.bfloat16)
    moment_new = jnp.dot(turned, right_basis, preferred_element_type=jnp.float32).astype(
        jnp.bfloat16
    )
    return (left_stat, right_statistic, left_basis, right_basis, moment_new)


def vacant(left_gram, right_gram, left_old, right_old, gradient, moment):
    blank = jnp.zeros_like(gradient)
    return (blank, blank, blank, blank, blank)


def local(grad_part, owner, moment, gram_left, gram_right, basis_left, basis_right):
    owner_count = lax.axis_size("mp")
    my_index = lax.axis_index("mp")
    my_group = lax.axis_index("dp")
    row_count = moment.shape[1]
    block_width = moment.shape[2]
    slot_count = gram_left.shape[2]
    my_table = lax.dynamic_index_in_dim(owner, my_group, 0, keepdims=False)
    onehot = slot_mapping(my_table, slot_count, owner_count)
    summed = lax.psum_scatter(
        grad_part[0].astype(jnp.float32).astype(jnp.bfloat16), "dp", scatter_dimension=0, tiled=True
    )
    grads, moments = (
        lax.all_to_all(pack_rows(onehot, summed), "mp", split_axis=1, concat_axis=1, tiled=True),
        lax.all_to_all(pack_rows(onehot, moment), "mp", split_axis=1, concat_axis=1, tiled=True),
    )
    my_load = jnp.sum(jnp.where(my_table == my_index, 1, 0))
    results = []
    for slot_index in range(slot_count):
        results.append(
            lax.cond(
                my_load > slot_index,
                refresh,
                vacant,
                gram_left[0, 0, slot_index],
                gram_right[0, 0, slot_index],
                basis_left[0, 0, slot_index],
                basis_right[0, 0, slot_index],
                grads[slot_index],
                moments[slot_index],
            )
        )
    stacked = [jnp.stack([result[which] for result in results])[None, None] for which in range(4)]
    turned_back = jnp.stack([result[4] for result in results])
    landed = lax.all_to_all(turned_back, "mp", split_axis=1, concat_axis=1, tiled=True)
    landed = landed.reshape(slot_count, owner_count, row_count, block_width)
    moment_new = jnp.einsum(
        "jso,sorc->jrc", onehot, landed, preferred_element_type=jnp.float32
    ).astype(jnp.bfloat16)
    return (stacked[0], stacked[1], stacked[2], stacked[3], moment_new)


def solution(mesh):
    return jax.shard_map(
        local,
        mesh=mesh,
        in_specs=(
            P("dp", None, "mp", None),
            P(),
            P("dp", "mp", None),
            P("dp", "mp", None, None, None),
            P("dp", "mp", None, None, None),
            P("dp", "mp", None, None, None),
            P("dp", "mp", None, None, None),
        ),
        out_specs=(
            P("dp", "mp", None, None, None),
            P("dp", "mp", None, None, None),
            P("dp", "mp", None, None, None),
            P("dp", "mp", None, None, None),
            P("dp", "mp", None),
        ),
        check_vma=False,
    )
```

profile of v0, /device:TPU:0, one launch (start us, length us, event | category | flops | bytes accessed | tf_op | source)
XLA Modules:
  0.0 754.5 jit_solution(554411982686204902)
XLA Ops:
  7.9 1.3 fusion.175
  10.4 2.0 copy.117
  12.4 7.3 all-to-all-start.1
  19.7 21.6 %reduce-scatter.2.cloned.1.call-done = bf16[6,64,512]{2,1,0:T(8,128)(2,1)} async-done(((bf16[24,64,512]{2,1,0:T(8,128)(2,1)}), bf16[6,64,512]{2,1,0:T(8,128)(2,1)}) %reduce-scatter.2.cloned.1.call-update) | async-done | bytes 393232 | tf_op jit(solution)/shard_map/reduce_scatter | solution.py:85
  41.3 1.5 convolution_convert_fusion.7
  43.2 2.0 copy.113
  45.5 5.3 all-to-all-start
  52.1 24.5 %all-to-all-done = bf16[2,512,512]{2,0,1:T(2,128)(2,1)} async-done(((bf16[2,512,512]{2,0,1:T(2,128)(2,1)}), bf16[2,512,512]{2,0,1:T(2,128)(2,1)}, u32[]{:S(2)}, u32[]{:S(2)}) %all-to-all-start) | async-done | bytes 1048608 | tf_op jit(solution)/shard_map/all_to_all | solution.py:89
  76.5 12.0 %conditional.3 = (bf16[1,512,512]{2,1,0:T(8,128)(2,1)}, bf16[1,512,512]{2,1,0:T(8,128)(2,1)S(1)}, bf16[1,512,512]{2,1,0:T(8,128)(2,1)}, bf16[1,512,512]{2,1,0:T(8,128)(2,1)}, bf16[1,512,512]{2,1,0:T(8,128)(2,1)S(1)}) conditional(s32[]{:T(128)} %convert_element_type.103, () %tuple.48, (bf16[1,1,2,512,512]{4,3,2,1,0:T(8,128)(2,1)}, ...), branch_computations={%region_13.16_spmd, %region_14.17_spmd} | conditional | flops 8205764096 | bytes 97002384 | solution.py:96
  88.6 3.2 copy.127
  91.8 302.1 %conditional.2 = (bf16[1,512,512]{2,1,0:T(8,128)(2,1)S(1)}, bf16[1,512,512]{2,1,0:T(8,128)(2,1)}, bf16[1,512,512]{2,1,0:T(8,128)(2,1)}, bf16[1,512,512]{2,1,0:T(8,128)(2,1)}, bf16[1,512,512]{2,1,0:T(8,128)(2,1)}) conditional(s32[]{:T(128)} %convert_element_type.100, () %tuple.46, (bf16[1,1,2,512,512]{4,3,2,1,0:T(8,128)(2,1)}, ...), branch_computations={%region_3.4_spmd, %region_4.15_spmd} | conditional | flops 8205764096 | bytes 105128880 | solution.py:96
  91.8 1.5 copy.118
  93.3 1.3 fusion.3
  94.6 1.3 fusion.4
  96.1 2.8 fusion.5
  98.9 1.5 fusion.26
  100.4 1.9 fusion.181
  103.8 11.7 %cholesky.534 = f32[128,128]{1,0:T(8,128)S(1)} custom-call(f32[128,128]{1,0:T(8,128)S(1)} %cholesky.759), custom_call_target="Cholesky" | custom-call | tf_op jit(solution)/shard_map/cond/branch_1_fun/jit(cholesky)/cholesky | solution.py:40
  115.7 9.8 %custom-call.39 = f32[1,128,128]{1,2,0:T(8,128)S(1)} custom-call(f32[1,128,128]{2,1,0:T(8,128)S(1)} %get-tuple-element.272), custom_call_target="InvertDiagBlocksLowerTriangular" | custom-call | tf_op jit(solution)/shard_map/cond/branch_1_fun/jit(cholesky)/cholesky | solution.py:40
  125.5 1.2 constant_dynamic-update-slice_fusion.3
  126.7 1.3 convolution_subtract_fusion.6
  128.0 11.9 %cholesky.553 = f32[128,128]{1,0:T(8,128)S(1)} custom-call(f32[128,128]{1,0:T(8,128)S(1)} %cholesky.763), custom_call_target="Cholesky" | custom-call | tf_op jit(solution)/shard_map/cond/branch_1_fun/jit(cholesky)/cholesky | solution.py:40
  139.9 9.8 %custom-call.40 = f32[1,128,128]{1,2,0:T(8,128)S(1)} custom-call(f32[1,128,128]{2,1,0:T(8,128)S(1)} %get-tuple-element.269), custom_call_target="InvertDiagBlocksLowerTriangular" | custom-call | tf_op jit(solution)/shard_map/cond/branch_1_fun/jit(cholesky)/cholesky | solution.py:40
  150.0 1.3 convolution_subtract_fusion.8
  151.3 11.7 %cholesky.574 = f32[128,128]{1,0:T(8,128)S(1)} custom-call(f32[128,128]{1,0:T(8,128)S(1)} %cholesky.768), custom_call_target="Cholesky" | custom-call | tf_op jit(solution)/shard_map/cond/branch_1_fun/jit(cholesky)/cholesky | solution.py:40
  163.0 9.8 %custom-call.41 = f32[1,128,128]{1,2,0:T(8,128)S(1)} custom-call(f32[1,128,128]{2,1,0:T(8,128)S(1)} %get-tuple-element.266), custom_call_target="InvertDiagBlocksLowerTriangular" | custom-call | tf_op jit(solution)/shard_map/cond/branch_1_fun/jit(cholesky)/cholesky | solution.py:40
  173.1 1.2 convolution_subtract_fusion.10
  174.3 12.1 %cholesky.591 = f32[128,128]{1,0:T(8,128)S(1)} custom-call(f32[128,128]{1,0:T(8,128)S(1)} %convolution_subtract_fusion.10), custom_call_target="Cholesky" | custom-call | tf_op jit(solution)/shard_map/cond/branch_1_fun/jit(cholesky)/cholesky | solution.py:40
  191.1 7.7 %while.9 = (s32[]{:T(128)}, f32[512,512]{1,0:T(8,128)S(1)}, s32[4,2]{0,1:T(2,128)S(1)}, f32[4,128,128]{2,1,0:T(8,128)S(1)}, s32[]{:T(128)}) while((s32[]{:T(128)}, f32[512,512]{1,0:T(8,128)S(1)}, s32[4,2]{0,1:T(2,128)S(1)}, f32[4,128,128]{2,1,0:T(8,128)S(1)}, s32[]{:T(128)}) %tuple.172), condition=%wide.while_cond.clone, body=%wide.while_body.clone.sunk | while | flops 2 | bytes 131189 | solution.py:41
  191.7 1.3 bitcast_dynamic-update-slice_fusion.11
  193.6 1.3 bitcast_dynamic-update-slice_fusion.11
  195.5 1.3 bitcast_dynamic-update-slice_fusion.11
  197.4 1.3 bitcast_dynamic-update-slice_fusion.11
  198.7 39.3 %custom-call.42 = f32[4,128,128]{1,2,0:T(8,128)S(1)} custom-call(f32[4,128,128]{2,1,0:T(8,128)S(1)} %get-tuple-element.124), custom_call_target="InvertDiagBlocksLowerTriangular" | custom-call | tf_op jit(solution)/shard_map/cond/branch_1_fun/jit(_solve_triangular)/triangular_solve | solution.py:41
  241.0 2.5 convolution_subtract_fusion.4
  244.4 1.9 fusion.180
  247.8 11.7 %cholesky.462 = f32[128,128]{1,0:T(8,128)S(1)} custom-call(f32[128,128]{1,0:T(8,128)S(1)} %cholesky.746), custom_call_target="Cholesky" | custom-call | tf_op jit(solution)/shard_map/cond/branch_1_fun/jit(cholesky)/cholesky | solution.py:40
  259.7 10.0 %custom-call.35 = f32[1,128,128]{1,2,0:T(8,128)S(1)} custom-call(f32[1,128,128]{2,1,0:T(8,128)S(1)} %get-tuple-element.262), custom_call_target="InvertDiagBlocksLowerTriangular" | custom-call | tf_op jit(solution)/shard_map/cond/branch_1_fun/jit(cholesky)/cholesky | solution.py:40
  269.7 1.2 constant_dynamic-update-slice_fusion.5
  270.9 1.3 convolution_subtract_fusion.7
  272.2 11.7 %cholesky.481 = f32[128,128]{1,0:T(8,128)S(1)} custom-call(f32[128,128]{1,0:T(8,128)S(1)} %cholesky.750), custom_call_target="Cholesky" | custom-call | tf_op jit(solution)/shard_map/cond/branch_1_fun/jit(cholesky)/cholesky | solution.py:40
  283.9 9.8 %custom-call.36 = f32[1,128,128]{1,2,0:T(8,128)S(1)} custom-call(f32[1,128,128]{2,1,0:T(8,128)S(1)} %get-tuple-element.259), custom_call_target="InvertDiagBlocksLowerTriangular" | custom-call | tf_op jit(solution)/shard_map/cond/branch_1_fun/jit(cholesky)/cholesky | solution.py:40
  294.0 1.3 convolution_subtract_fusion.9
  295.3 11.7 %cholesky.502 = f32[128,128]{1,0:T(8,128)S(1)} custom-call(f32[128,128]{1,0:T(8,128)S(1)} %cholesky.755), custom_call_target="Cholesky" | custom-call | tf_op jit(solution)/shard_map/cond/branch_1_fun/jit(cholesky)/cholesky | solution.py:40
  307.1 10.0 %custom-call.37 = f32[1,128,128]{1,2,0:T(8,128)S(1)} custom-call(f32[1,128,128]{2,1,0:T(8,128)S(1)} %get-tuple-element.256), custom_call_target="InvertDiagBlocksLowerTriangular" | custom-call | tf_op jit(solution)/shard_map/cond/branch_1_fun/jit(cholesky)/cholesky | solution.py:40
  317.3 1.2 convolution_subtract_fusion.11
  318.5 11.7 %cholesky.519 = f32[128,128]{1,0:T(8,128)S(1)} custom-call(f32[128,128]{1,0:T(8,128)S(1)} %convolution_subtract_fusion.11), custom_call_target="Cholesky" | custom-call | tf_op jit(solution)/shard_map/cond/branch_1_fun/jit(cholesky)/cholesky | solution.py:40
  334.9 7.7 %while.8 = (s32[]{:T(128)}, f32[512,512]{1,0:T(8,128)S(1)}, s32[4,2]{0,1:T(2,128)S(1)}, f32[4,128,128]{2,1,0:T(8,128)S(1)}, s32[]{:T(128)}) while((s32[]{:T(128)}, f32[512,512]{1,0:T(8,128)S(1)}, s32[4,2]{0,1:T(2,128)S(1)}, f32[4,128,128]{2,1,0:T(8,128)S(1)}, s32[]{:T(128)}) %tuple.185), condition=%wide.while_cond, body=%wide.while_body.sunk | while | flops 2 | bytes 131189 | solution.py:41
  335.5 1.3 bitcast_dynamic-update-slice_fusion.10
  337.4 1.3 bitcast_dynamic-update-slice_fusion.10
  339.3 1.3 bitcast_dynamic-update-slice_fusion.10
  341.2 1.3 bitcast_dynamic-update-slice_fusion.10
  342.5 39.6 %custom-call.38 = f32[4,128,128]{1,2,0:T(8,128)S(1)} custom-call(f32[4,128,128]{2,1,0:T(8,128)S(1)} %get-tuple-element.123), custom_call_target="InvertDiagBlocksLowerTriangular" | custom-call | tf_op jit(solution)/shard_map/cond/branch_1_fun/jit(_solve_triangular)/triangular_solve | solution.py:41
  384.6 1.3 fusion.64
  385.9 1.5 convolution_subtract_fusion.5
  387.4 1.3 fusion.63
  388.7 2.7 fusion.6
  391.5 1.0 copy.153
  393.9 1.9 copy.126
  395.8 3.2 pad_maximum_fusion
  399.1 322.6 %all-to-all-start.2 = ((bf16[2,512,512]{2,0,1:T(2,128)(2,1)}), bf16[2,512,512]{2,0,1:T(2,128)(2,1)S(1)}, u32[]{:S(2)}, u32[]{:S(2)}) async-start(bf16[2,512,512]{2,0,1:T(2,128)(2,1)} %pad_maximum_fusion), calls=%async_computation.3 | async-start | bytes 2097152 | tf_op jit(solution)/shard_map/all_to_all | solution.py:110
  721.7 2.8 maximum_bitcast_fusion
  724.4 2.9 maximum_bitcast_fusion.2
  727.3 18.4 %all-to-all-done.2 = bf16[2,512,512]{2,0,1:T(2,128)(2,1)S(1)} async-done(((bf16[2,512,512]{2,0,1:T(2,128)(2,1)}), bf16[2,512,512]{2,0,1:T(2,128)(2,1)S(1)}, u32[]{:S(2)}, u32[]{:S(2)}) %all-to-all-start.2) | async-done | bytes 1048608 | tf_op jit(solution)/shard_map/all_to_all | solution.py:110
  (129 shorter events, 27.6 us)
Async XLA Ops:
  7.2 2.3 copy-start.31
  7.2 34.1 %reduce-scatter.2.cloned.1.call-start = ((), (), s32[]{:S(2)}) async-start(), calls=%async_computation.4 | async-start | bytes 1966080 | tf_op jit(solution)/shard_map/reduce_scatter | solution.py:85
  12.4 33.0 %all-to-all-start.1 = ((bf16[2,512,512]{2,0,1:T(2,128)(2,1)}), bf16[2,512,512]{2,0,1:T(2,128)(2,1)S(1)}, u32[]{:S(2)}, u32[]{:S(2)}) async-start(bf16[2,512,512]{2,0,1:T(2,128)(2,1)} %copy.117), calls=%async_computation.2 | async-start | bytes 2097152 | tf_op jit(solution)/shard_map/all_to_all | solution.py:90
  45.5 31.0 %all-to-all-start = ((bf16[2,512,512]{2,0,1:T(2,128)(2,1)}), bf16[2,512,512]{2,0,1:T(2,128)(2,1)}, u32[]{:S(2)}, u32[]{:S(2)}) async-start(bf16[2,512,512]{2,0,1:T(2,128)(2,1)} %copy.113), calls=%async_computation.1 | async-start | bytes 2097152 | tf_op jit(solution)/shard_map/all_to_all | solution.py:89
  88.6 3.2 copy-start.25
  88.6 3.2 copy-start.2
  91.8 1.5 copy-start.36
  93.3 1.3 copy-start.38
  96.0 2.8 copy-start.29
  102.8 1.0 copy-start.14
  198.7 40.8 %copy-start.11 = (f32[512,512]{1,0:T(8,128)}, f32[512,512]{1,0:T(8,128)S(1)}, u32[]{:S(2)}) copy-start(f32[512,512]{1,0:T(8,128)S(1)} %get-tuple-element.518) | copy-start | bytes 3145732 | tf_op jit(solution)/shard_map/cond
  239.5 4.0 copy-start.9
  240.5 3.4 copy-start.4
  240.5 3.4 copy-start.28
  241.0 3.4 copy-start.18
  246.8 1.0 copy-start.15
  382.1 1.5 copy-start.34
  384.6 4.1 copy-start.10
  384.6 4.1 copy-start.19
  385.9 1.5 copy-start.23
  388.7 2.7 copy-start.24
  391.4 1.1 copy-start.20
  391.5 2.1 copy-start.5
  393.9 2.0 copy-start.6
  399.1 322.6 %copy-start.3 = (bf16[1,512,512]{2,1,0:T(8,128)(2,1)S(1)}, bf16[1,512,512]{2,1,0:T(8,128)(2,1)}, u32[]{:S(2)}) copy-start(bf16[1,512,512]{2,1,0:T(8,128)(2,1)} %copy-done.2) | copy-start | bytes 1572868
  399.1 346.6 %all-to-all-start.2 = ((bf16[2,512,512]{2,0,1:T(2,128)(2,1)}), bf16[2,512,512]{2,0,1:T(2,128)(2,1)S(1)}, u32[]{:S(2)}, u32[]{:S(2)}) async-start(bf16[2,512,512]{2,0,1:T(2,128)(2,1)} %pad_maximum_fusion), calls=%async_computation.3 | async-start | bytes 2097152 | tf_op jit(solution)/shard_map/all_to_all | solution.py:110
  721.6 2.8 copy-start.26
Sparse Core Ops, SparseCore 0:
  10.5 30.7 reduce-scatter.1
where the time goes:
time: 761 us; the launch traced here: 754 us
  starting transfers between devices  335 us (44%)
  other arithmetic  248 us (33%)
  waiting for transfers between devices  65.4 us (9%)
  matrix products  39.7 us (5%)
  local copies, waits for them, and re-layouts  35.2 us (5%)
  between operations  15.8 us (2%)
  loops' own time  15.6 us (2%)
    all_to_all x1, starting transfers between devices, local(): lax.all_to_all(turned_back, 'mp', split_axis=1, concat_axis=1, tiled=True)  323 us
    another operation x28, other arithmetic, orthonormal(): factor = jnp.linalg.cholesky(square)  158 us
    another operation x5, other arithmetic, orthonormal(): jax.scipy.linalg.solve_triangular(factor, matrix_product.T, lower=True)  79.1 us
    all_to_all x1, waiting for transfers between devices, local(): lax.all_to_all(pack_rows(onehot, summed), 'mp', split_axis=1, concat_axis...  24.5 us
    reduce_scatter x1, waiting for transfers between devices, local(): lax.psum_scatter(grad_part[0].astype(jnp.float32).astype(jnp.bfloat16), '...  21.6 us
    all_to_all x1, waiting for transfers between devices, local(): lax.all_to_all(turned_back, 'mp', split_axis=1, concat_axis=1, tiled=True)  18.4 us
    another operation x2, loops' own time, local(): lax.cond(my_load > slot_index, refresh, vacant, gram_left[0, 0, slot_inde...  15.4 us
  transfers between devices with their start and end apart: 4, of which 4 were waited for; matrix products, arithmetic and copies ran while one was open for 2% of the time, Pallas kernels for 0%

commit v1 on v0

--- a/solution.py
+++ b/solution.py
@@ -1,6 +1,10 @@
+import functools
+
 import jax
 import jax.numpy as jnp
 from jax import lax
+from jax.experimental import pallas as pl
+from jax.experimental.pallas import tpu as pltpu
 from jax.sharding import PartitionSpec as P
 
 gram_decay = 0.85
@@ -30,47 +34,110 @@
     )
 
 
-def orthonormal(matrix_product):
-    square = jnp.dot(
-        matrix_product.T,
-        matrix_product,
-        precision=lax.Precision.HIGHEST,
-        preferred_element_type=jnp.float32,
-    )
-    factor = jnp.linalg.cholesky(square)
-    solved = jax.scipy.linalg.solve_triangular(factor, matrix_product.T, lower=True)
-    return solved.T.astype(jnp.bfloat16)
+HI = lax.Precision.HIGHEST
+
+def _nt(a, b):
+    return lax.dot_general(a, b, (((1,), (1,)), ((), ())), precision=HI,
+                           preferred_element_type=jnp.float32)
+
+def _orth_kernel(s_ref, p_ref, q_ref, a_ref, m_ref, w_ref, qf_ref, *, nb):
+    bsz, n, _ = s_ref.shape
+    kb = n // nb
+    a_ref[...] = s_ref[...]
+    eye = (lax.broadcasted_iota(jnp.int32, (nb, nb), 0)
+           == lax.broadcasted_iota(jnp.int32, (nb, nb), 1)).astype(jnp.float32)
+    lane = lax.broadcasted_iota(jnp.int32, (1, 1, 2 * nb), 2)
+    lane_l = lax.broadcasted_iota(jnp.int32, (1, 1, nb), 2)
+    sub = lax.broadcasted_iota(jnp.int32, (1, nb, 1), 1)
+    for k in range(kb):
+        k0 = k * nb
+        m_ref[:, :, :nb] = a_ref[:, k0:k0 + nb, k0:k0 + nb]
+        m_ref[:, :, nb:] = jnp.broadcast_to(eye, (bsz, nb, nb))
+
+        def step(j, carry):
+            row = m_ref[:, pl.ds(j, 1), :]
+            piv = jnp.sum(jnp.where(lane == j, row, 0.0), axis=-1, keepdims=True)
+            inv_s = 1.0 / jnp.sqrt(piv)
+            scaled = row * inv_s
+            left = m_ref[:, :, :nb]
+            col = jnp.sum(jnp.where(lane_l == j, left, 0.0), axis=-1, keepdims=True) * inv_s
+            col = jnp.where(sub > j, col, 0.0)
+            m_ref[...] = m_ref[...] - col * scaled
+            m_ref[:, pl.ds(j, 1), :] = scaled
+            return carry
+
+        lax.fori_loop(0, nb, step, 0)
+        w_ref[:, k] = m_ref[:, :, nb:]
+        if k < kb - 1:
+            for b in range(bsz):
+                panel = _nt(a_ref[b, k0 + nb:, k0:k0 + nb], w_ref[b, k])
+                a_ref[b, k0 + nb:, k0:k0 + nb] = panel
+                a_ref[b, k0 + nb:, k0 + nb:] = a_ref[b, k0 + nb:, k0 + nb:] - _nt(panel, panel)
+    for k in range(kb):
+        k0 = k * nb
+        for b in range(bsz):
+            rhs = p_ref[b, :, k0:k0 + nb]
+            if k > 0:
+                rhs = rhs - _nt(qf_ref[b, :, :k0], a_ref[b, k0:k0 + nb, :k0])
+            qf_ref[b, :, k0:k0 + nb] = _nt(rhs, w_ref[b, k])
+    q_ref[...] = qf_ref[...].astype(q_ref.dtype)
 
 
-def refresh(left_gram, right_gram, left_old, right_old, gradient, moment):
-    block_width = gradient.shape[0]
-    outer_left = jnp.dot(gradient, gradient.T, preferred_element_type=jnp.float32)
-    outer_right = jnp.dot(gradient.T, gradient, preferred_element_type=jnp.float32)
+def orth_batch(square, power, nb=128):
+    bsz, n, _ = square.shape
+    vmem = pltpu.VMEM
+    return pl.pallas_call(
+        functools.partial(_orth_kernel, nb=nb),
+        out_shape=jax.ShapeDtypeStruct((bsz, n, n), jnp.bfloat16),
+        in_specs=[pl.BlockSpec(memory_space=vmem)] * 2,
+        out_specs=pl.BlockSpec(memory_space=vmem),
+        scratch_shapes=[
+            vmem((bsz, n, n), jnp.float32),
+            vmem((bsz, nb, 2 * nb), jnp.float32),
+            vmem((bsz, n // nb, nb, nb), jnp.float32),
+            vmem((bsz, n, n), jnp.float32),
+        ],
+        compiler_params=pltpu.CompilerParams(vmem_limit_bytes=60 * 1024 * 1024),
+    )(square, power)
+
+
+def refresh_all(left_gram, right_gram, left_old, right_old, gradient, moment):
+    block_width = gradient.shape[-1]
+    slots = gradient.shape[0]
+    outer_left = jnp.einsum("sij,skj->sik", gradient, gradient, preferred_element_type=jnp.float32)
+    outer_right = jnp.einsum("sji,sjk->sik", gradient, gradient, preferred_element_type=jnp.float32)
     left_stat = (
         gram_decay * left_gram.astype(jnp.float32) + (1.0 - gram_decay) / block_width * outer_left
     ).astype(jnp.bfloat16)
     right_statistic = (
         gram_decay * right_gram.astype(jnp.float32) + (1.0 - gram_decay) / block_width * outer_right
     ).astype(jnp.bfloat16)
-    left_basis = orthonormal(jnp.dot(left_stat, left_old, preferred_element_type=jnp.float32))
-    right_basis = orthonormal(
-        jnp.dot(right_statistic, right_old, preferred_element_type=jnp.float32)
+    left_power = jnp.einsum("sij,sjk->sik", left_stat, left_old, preferred_element_type=jnp.float32)
+    right_power = jnp.einsum(
+        "sij,sjk->sik", right_statistic, right_old, preferred_element_type=jnp.float32
     )
-    restored = jnp.dot(left_old, moment, preferred_element_type=jnp.float32).astype(jnp.bfloat16)
+    power = jnp.concatenate([left_power, right_power], axis=0)
+    square = jnp.einsum(
+        "bji,bjk->bik", power, power, precision=lax.Precision.HIGHEST,
+        preferred_element_type=jnp.float32,
+    )
+    basis = orth_batch(square, power)
+    left_basis, right_basis = basis[:slots], basis[slots:]
+    restored = jnp.einsum(
+        "sij,sjk->sik", left_old, moment, preferred_element_type=jnp.float32
+    ).astype(jnp.bfloat16)
     mixed = (
-        moment_decay * jnp.dot(restored, right_old.T, preferred_element_type=jnp.float32)
+        moment_decay
+        * jnp.einsum("sij,skj->sik", restored, right_old, preferred_element_type=jnp.float32)
         + (1.0 - moment_decay) * gradient.astype(jnp.float32)
     ).astype(jnp.bfloat16)
-    turned = jnp.dot(left_basis.T, mixed, preferred_element_type=jnp.float32).astype(jnp.bfloat16)
-    moment_new = jnp.dot(turned, right_basis, preferred_element_type=jnp.float32).astype(
-        jnp.bfloat16
-    )
+    turned = jnp.einsum(
+        "sji,sjk->sik", left_basis, mixed, preferred_element_type=jnp.float32
+    ).astype(jnp.bfloat16)
+    moment_new = jnp.einsum(
+        "sij,sjk->sik", turned, right_basis, preferred_element_type=jnp.float32
+    ).astype(jnp.bfloat16)
     return (left_stat, right_statistic, left_basis, right_basis, moment_new)
-
-
-def vacant(left_gram, right_gram, left_old, right_old, gradient, moment):
-    blank = jnp.zeros_like(gradient)
-    return (blank, blank, blank, blank, blank)
 
 
 def local(grad_part, owner, moment, gram_left, gram_right, basis_left, basis_right):
@@ -90,23 +157,13 @@
         lax.all_to_all(pack_rows(onehot, moment), "mp", split_axis=1, concat_axis=1, tiled=True),
     )
     my_load = jnp.sum(jnp.where(my_table == my_index, 1, 0))
-    results = []
-    for slot_index in range(slot_count):
-        results.append(
-            lax.cond(
-                my_load > slot_index,
-                refresh,
-                vacant,
-                gram_left[0, 0, slot_index],
-                gram_right[0, 0, slot_index],
-                basis_left[0, 0, slot_index],
-                basis_right[0, 0, slot_index],
-                grads[slot_index],
-                moments[slot_index],
-            )
-        )
-    stacked = [jnp.stack([result[which] for result in results])[None, None] for which in range(4)]
-    turned_back = jnp.stack([result[4] for result in results])
+    results = refresh_all(
+        gram_left[0, 0], gram_right[0, 0], basis_left[0, 0], basis_right[0, 0], grads, moments
+    )
+    live = (lax.broadcasted_iota(jnp.int32, (slot_count, 1, 1), 0) < my_load)
+    results = [jnp.where(live, r, jnp.zeros_like(r)) for r in results]
+    stacked = [results[which][None, None] for which in range(4)]
+    turned_back = results[4]
     landed = lax.all_to_all(turned_back, "mp", split_axis=1, concat_axis=1, tiled=True)
     landed = landed.reshape(slot_count, owner_count, row_count, block_width)
     moment_new = jnp.einsum(

time: 761 us -> 252 us (0.33)
  starting transfers between devices: 335 us -> 15.7 us
  other arithmetic: 248 us -> 8.33 us
  Pallas kernels: 0 us -> 104 us
  local copies, waits for them, and re-layouts: 35.2 us -> 9 us
  matrix products: 39.7 us -> 23.6 us
  loops' own time: 15.6 us -> 0 us
  waiting for transfers between devices: 65.4 us -> 76.6 us
    all_to_all x1, starting transfers between devices: 323 us -> 5.72 us  [local(): lax.all_to_all(turned_back, 'mp', split_axis=1, concat_axis=1, tiled=True)]
    another operation x36 -> x0, other arithmetic: 240 us -> none  [the longest x28 158 us: orthonormal(): factor = jnp.linalg.cholesky(square)]
    pallas_call x0 -> x1, Pallas kernels: none -> 104 us  [orth_batch(): pl.pallas_call(functools.partial(_orth_kernel, nb=nb), out_shape=jax.Shap...]
    another operation x26 -> x0, matrix products: 23.2 us -> none  [the longest x14 12.2 us: orthonormal(): jax.scipy.linalg.solve_triangular(factor, matrix_product.T, lower=True)]
    another operation x42 -> x0, local copies, waits for them, and re-layouts: 19.7 us -> none  [the longest x27 15.2 us: orthonormal(): jax.scipy.linalg.solve_triangular(factor, matrix_product.T, lower=True)]
    another operation x4 -> x0, loops' own time: 15.6 us -> none  [the longest x2 15.4 us: local(): lax.cond(my_load > slot_index, refresh, vacant, gram_left[0, 0, slot_inde...]
    reduce_scatter x1, waiting for transfers between devices: 21.6 us -> 31.8 us  [local(): lax.psum_scatter(grad_part[0].astype(jnp.float32).astype(jnp.bfloat16), '...]
    cond x38 -> x0, local copies, waits for them, and re-layouts: 9.24 us -> none  [the longest x4 7.18 us: local(): lax.cond(my_load > slot_index, refresh, vacant, gram_left[0, 0, slot_inde...]
  transfers between devices with their start and end apart: 4 -> 4, of which waited for: 4 -> 3; matrix products, arithmetic and copies ran while one was open for 2% -> 9% of each run, Pallas kernels for 0% -> 41%
where the time goes in v1:
time: 252 us
  Pallas kernels  104 us (41%)
  waiting for transfers between devices  76.6 us (30%)
  matrix products  23.6 us (9%)
  starting transfers between devices  15.7 us (6%)
  between operations  14.2 us (6%)
  local copies, waits for them, and re-layouts  9 us (4%)
  other arithmetic  8.33 us (3%)
    pallas_call x1, Pallas kernels, orth_batch(): pl.pallas_call(functools.partial(_orth_kernel, nb=nb), out_shape=jax.Shap...  104 us
    reduce_scatter x1, waiting for transfers between devices, local(): lax.psum_scatter(grad_part[0].astype(jnp.float32).astype(jnp.bfloat16), '...  31.8 us
    all_to_all x1, waiting for transfers between devices, local(): lax.all_to_all(pack_rows(onehot, summed), 'mp', split_axis=1, concat_axis...  22.7 us
    all_to_all x1, waiting for transfers between devices, local(): lax.all_to_all(turned_back, 'mp', split_axis=1, concat_axis=1, tiled=True)  21.4 us
    dot_general x1, matrix products, refresh_all(): jnp.einsum('bji,bjk->bik', power, power, precision=lax.Precision.HIGHEST,...  8.93 us
    all_to_all x1, starting transfers between devices, local(): lax.all_to_all(turned_back, 'mp', split_axis=1, concat_axis=1, tiled=True)  5.72 us
    all_to_all x1, starting transfers between devices, local(): lax.all_to_all(pack_rows(onehot, summed), 'mp', split_axis=1, concat_axis...  5.52 us
  transfers between devices with their start and end apart: 4, of which 3 were waited for; matrix products, arithmetic and copies ran while one was open for 9% of the time, Pallas kernels for 41%

profile of v1, /device:TPU:0, one launch (start us, length us, event | category | flops | bytes accessed | tf_op | source)
XLA Modules:
  0.0 251.7 jit_solution(14894921894244005820)
XLA Ops:
  7.2 0.0 copy-start
  7.2 0.0 reduce-scatter.2.cloned.1.call-start
  7.2 0.7 reduce-scatter.2.cloned.1.call-update
  7.9 1.3 fusion.29
  9.2 0.2 select_reduce_fusion
  9.4 0.1 iota_compare_fusion.1
  9.5 31.8 %reduce-scatter.2.cloned.1.call-done = bf16[6,64,512]{2,1,0:T(8,128)(2,1)} async-done(((bf16[24,64,512]{2,1,0:T(8,128)(2,1)}), bf16[6,64,512]{2,1,0:T(8,128)(2,1)}) %reduce-scatter.2.cloned.1.call-update) | async-done | bytes 393232 | tf_op jit(solution)/shard_map/reduce_scatter | solution.py:152
  41.3 1.5 convolution_convert_fusion.4
  42.9 0.3 copy.72
  43.2 0.0 copy-start.6
  43.2 2.0 copy.73
  45.2 5.5 %all-to-all-start = ((bf16[2,512,512]{2,0,1:T(2,128)(2,1)}), bf16[2,512,512]{2,0,1:T(2,128)(2,1)S(1)}, u32[]{:S(2)}, u32[]{:S(2)}) async-start(bf16[2,512,512]{2,0,1:T(2,128)(2,1)} %copy.73), calls=%async_computation.1 | async-start | bytes 2097152 | tf_op jit(solution)/shard_map/all_to_all | solution.py:156
  50.8 0.0 copy-done.6
  50.8 0.5 convolution_convert_fusion.3
  51.3 0.3 copy.81
  51.6 0.0 copy-start.7
  51.7 2.0 copy.82
  53.7 22.7 %all-to-all-done = bf16[2,512,512]{2,0,1:T(2,128)(2,1)S(1)} async-done(((bf16[2,512,512]{2,0,1:T(2,128)(2,1)}), bf16[2,512,512]{2,0,1:T(2,128)(2,1)S(1)}, u32[]{:S(2)}, u32[]{:S(2)}) %all-to-all-start) | async-done | bytes 1048608 | tf_op jit(solution)/shard_map/all_to_all | solution.py:156
  76.4 0.0 copy-start.4
  76.4 4.4 %all-to-all-start.1 = ((bf16[2,512,512]{2,0,1:T(2,128)(2,1)}), bf16[2,512,512]{2,0,1:T(2,128)(2,1)}, u32[]{:S(2)}, u32[]{:S(2)}) async-start(bf16[2,512,512]{2,0,1:T(2,128)(2,1)} %copy.82), calls=%async_computation.2 | async-start | bytes 2097152 | tf_op jit(solution)/shard_map/all_to_all | solution.py:157
  80.9 0.7 iota_compare_fusion.3
  81.5 0.0 copy-done.7
  81.5 0.0 copy-start.8
  81.5 0.8 fusion.1
  82.3 0.0 copy-done.4
  82.3 0.4 copy-done.8
  82.8 0.0 copy-start.2
  82.8 0.8 fusion
  83.6 0.0 copy-done
  83.6 0.0 copy-start.3
  83.6 0.0 copy-start.5
  83.6 0.7 fusion.7
  84.3 0.0 copy-done.2
  84.3 0.2 copy-done.3
  84.6 0.6 copy-done.5
  85.2 0.7 fusion.11
  85.9 8.9 %fusion.30.s_ref = f32[4,512,512]{2,1,0:T(8,128)} fusion(f32[2,512,512]{2,1,0:T(8,128)S(1)} %fusion.7, f32[2,512,512]{2,1,0:T(8,128)S(1)} %fusion.11), kind=kOutput, calls=%fused_computation.51 | convolution fusion | flops 6443499520 | bytes 8388608 | tf_op jit(solution)/shard_map/bji,bjk->bik/dot_general | solution.py:120
  94.9 2.4 pad_maximum_fusion.p_ref
  97.3 104.2 %shard_map.110 = bf16[4,512,512]{2,1,0:T(8,128)(2,1)} custom-call(f32[4,512,512]{2,1,0:T(8,128)} %fusion.30.s_ref, f32[4,512,512]{2,1,0:T(8,128)} %pad_maximum_fusion.p_ref), custom_call_target="tpu_custom_call" | custom-call | tf_op jit(solution)/shard_map/pallas_call | solution.py:89
  201.5 0.0 copy-start.1
  201.5 0.0 all-to-all-done.1
  201.5 4.5 %add_convert_fusion = bf16[2,512,512]{2,1,0:T(8,128)(2,1)} fusion(bf16[1,1,2,512,512]{4,3,2,1,0:T(8,128)(2,1)S(1)} %copy-done, bf16[1,1,2,512,512]{4,3,2,1,0:T(8,128)(2,1)} %param.12, bf16[2,512,512]{2,0,1:T(2,128)(2,1)} %all-to-all-done.1, bf16[2,512,512]{2,0,1:T(2,128)(2,1)} %copy-done.4), kind=kOutput, calls=%fused_computation.5 | convolution fusion | flops 1076887552 | bytes 5242880 | tf_op jit(solution)/shard_map/sij,skj->sik/dot_general | solution.py:131
  206.0 0.0 copy-done.1
  206.0 2.4 convolution_convert_fusion
  208.4 0.7 fusion.2
  209.1 2.1 copy.87
  211.2 5.7 %all-to-all-start.2 = ((bf16[2,512,512]{2,0,1:T(2,128)(2,1)}), bf16[2,512,512]{2,0,1:T(2,128)(2,1)}, u32[]{:S(2)}, u32[]{:S(2)}) async-start(bf16[2,512,512]{2,0,1:T(2,128)(2,1)} %copy.87), calls=%async_computation.3 | async-start | bytes 2097152 | tf_op jit(solution)/shard_map/all_to_all | solution.py:167
  216.9 3.7 %select_bitcast_fusion = (bf16[1,1,2,512,512]{4,3,2,1,0:T(8,128)(2,1)}, bf16[1,1,2,512,512]{4,3,2,1,0:T(8,128)(2,1)}, bf16[1,1,2,512,512]{4,3,2,1,0:T(8,128)(2,1)}, bf16[1,1,2,512,512]{4,3,2,1,0:T(8,128)(2,1)}) fusion(pred[2]{0:T(512)(128)(4,1)S(1)} %iota_compare_fusion.3, bf16[4,512,512]{2,1,0:T(8,128)(2,1)S(1)} %copy-done.1, ...), kind=kLoop, calls=%fused_computation.24 | loop fusion | flops 2097152 | bytes 8388610 | tf_op jit(solution)/shard_map/broadcast_in_dim | solution.py:165
  220.6 21.4 %all-to-all-done.2 = bf16[2,512,512]{2,0,1:T(2,128)(2,1)} async-done(((bf16[2,512,512]{2,0,1:T(2,128)(2,1)}), bf16[2,512,512]{2,0,1:T(2,128)(2,1)}, u32[]{:S(2)}, u32[]{:S(2)}) %all-to-all-start.2) | async-done | bytes 1048608 | tf_op jit(solution)/shard_map/all_to_all | solution.py:167
  242.0 2.0 fusion.3
  244.0 0.9 copy.90
  (1 shorter events, 0.0 us)
Async XLA Ops:
  7.2 76.4 %copy-start = (bf16[1,1,2,512,512]{4,3,2,1,0:T(8,128)(2,1)S(1)}, bf16[1,1,2,512,512]{4,3,2,1,0:T(8,128)(2,1)}, u32[]{:S(2)}) copy-start(bf16[1,1,2,512,512]{4,3,2,1,0:T(8,128)(2,1)} %param.13) | copy-start | bytes 3145732
  7.2 34.1 %reduce-scatter.2.cloned.1.call-start = ((), (), s32[]{:S(2)}) async-start(), calls=%async_computation.4 | async-start | bytes 1966080 | tf_op jit(solution)/shard_map/reduce_scatter | solution.py:152
  43.2 7.6 %copy-start.6 = (bf16[6,64,512]{2,1,0:T(8,128)(2,1)S(1)}, bf16[6,64,512]{2,1,0:T(8,128)(2,1)}, u32[]{:S(2)}) copy-start(bf16[6,64,512]{2,1,0:T(8,128)(2,1)} %param.9) | copy-start | bytes 1179652
  45.2 31.2 %all-to-all-start = ((bf16[2,512,512]{2,0,1:T(2,128)(2,1)}), bf16[2,512,512]{2,0,1:T(2,128)(2,1)S(1)}, u32[]{:S(2)}, u32[]{:S(2)}) async-start(bf16[2,512,512]{2,0,1:T(2,128)(2,1)} %copy.73), calls=%async_computation.1 | async-start | bytes 2097152 | tf_op jit(solution)/shard_map/all_to_all | solution.py:156
  51.6 29.9 %copy-start.7 = (bf16[1,1,2,512,512]{4,3,2,1,0:T(8,128)(2,1)S(1)}, bf16[1,1,2,512,512]{4,3,2,1,0:T(8,128)(2,1)}, u32[]{:S(2)}) copy-start(bf16[1,1,2,512,512]{4,3,2,1,0:T(8,128)(2,1)} %param.10) | copy-start | bytes 3145732
  76.4 5.9 %copy-start.4 = (bf16[2,512,512]{2,0,1:T(2,128)(2,1)}, bf16[2,512,512]{2,0,1:T(2,128)(2,1)S(1)}, u32[]{:S(2)}) copy-start(bf16[2,512,512]{2,0,1:T(2,128)(2,1)S(1)} %all-to-all-done) | copy-start | bytes 3145732
  76.4 125.1 %all-to-all-start.1 = ((bf16[2,512,512]{2,0,1:T(2,128)(2,1)}), bf16[2,512,512]{2,0,1:T(2,128)(2,1)}, u32[]{:S(2)}, u32[]{:S(2)}) async-start(bf16[2,512,512]{2,0,1:T(2,128)(2,1)} %copy.82), calls=%async_computation.2 | async-start | bytes 2097152 | tf_op jit(solution)/shard_map/all_to_all | solution.py:157
  81.5 1.2 copy-start.8
  82.8 1.6 copy-start.2
  83.6 1.0 copy-start.3
  83.6 1.6 copy-start.5
  201.5 4.5 %copy-start.1 = (bf16[4,512,512]{2,1,0:T(8,128)(2,1)S(1)}, bf16[4,512,512]{2,1,0:T(8,128)(2,1)}, u32[]{:S(2)}) copy-start(bf16[4,512,512]{2,1,0:T(8,128)(2,1)} %shard_map.110) | copy-start | bytes 6291460
  211.2 30.8 %all-to-all-start.2 = ((bf16[2,512,512]{2,0,1:T(2,128)(2,1)}), bf16[2,512,512]{2,0,1:T(2,128)(2,1)}, u32[]{:S(2)}, u32[]{:S(2)}) async-start(bf16[2,512,512]{2,0,1:T(2,128)(2,1)} %copy.87), calls=%async_computation.3 | async-start | bytes 2097152 | tf_op jit(solution)/shard_map/all_to_all | solution.py:167
Sparse Core Ops, SparseCore 0:
  10.5 30.7 reduce-scatter.1
